TPU v7x, 32 devices: a whole 2x2x4 slice. The times are simulated.
32 devices in a mesh: groups: 2 (over y), dp: 4 (over z), mp: 4 (over x, core).
Axes of the slice: x: 2, y: 2, z: 4, core: 2. Of those that a mesh axis runs over, the one named last changes fastest.
Arguments:
- latents: bfloat16 [256, 640, 64], P(('groups', 'dp'), 'mp'), parts along dimension 0
- modulation: bfloat16 [256, 2, 640], P(('groups', 'dp'), None, 'mp'), parts along dimension 0, may hold values from -3 to 3
- first_kernel: bfloat16 [640, 9, 640], P('dp', None, 'mp'), may hold values from -0.078125 to 0.078125
- second_kernel: bfloat16 [640, 9, 640], P('dp', None, 'mp'), may hold values from -0.078125 to 0.078125
- encoder_cache: bfloat16 [336, 1280, 128], P(('groups', 'dp'), 'mp'), parts along dimension 0
- query_weight: bfloat16 [640, 640], P('dp'), may hold values from -0.25 to 0.25
- output_weight: bfloat16 [640, 640], P('dp'), may hold values from -0.25 to 0.25
- kept_prompt_list: int32 [256], P('groups'), parts along dimension 0, may hold values from 0 to 167, as said below
- destination: int32 [256], P('groups'), parts along dimension 0, may hold values from 0 to 3, as said below
- lengths: int32 [336], P('groups'), parts along dimension 0, may hold values from 1 to 128, 10752 in all
Outputs:
- level_out: bfloat16 [256, 640, 64], P(('groups', 'dp'), 'mp'), parts along dimension 0
There are 2 independent parts, one for each index of `groups`. A program takes and returns all parts, laid end to end along the dimension named above; an argument that names none is the same for every part. Nothing has to cross between parts.
Inputs may be any that keep to these rules, and one draw needn't show every extreme that they name: `kept_prompt_list`: entries o * 32 to o * 32 + 31 belong to owner o: distinct ids of its prompts o * 42 to o * 42 + 41. `destination`: names the shard of each survivor; every shard receives exactly 32 survivors, one owner sends at most 16 survivors to one shard, and every owner sends exactly 16 to some shard.
All inputs are finite; a program needn't handle non-finite values.
Results may differ from a plain program's by a relative error of at most 0.0055.
Values may be sent and summed in bfloat16 or wider, within the bound.
No kernel may reach another device: no remote copies, remote signals or barrier semaphores. Data moves between devices by JAX's collectives and lax.ppermute only.
A program may use at most 64 MiB of HBM per device.

v0:
```python
import jax
import jax.numpy as jnp
from jax import lax
from jax.sharding import PartitionSpec as P

C = 640
GROUPS = 32
HEAD = 64
SIDE = 8
EPSILON = 1e-05
MASKED = -1e30


def norm_groups(values, group_width):
    field_shape = values.shape
    grouped = values.reshape(
        field_shape[0], field_shape[1] // group_width, group_width, field_shape[2]
    )
    center = grouped - jnp.mean(grouped, axis=(2, 3), keepdims=True)
    spread = jnp.mean(center * center, axis=(2, 3), keepdims=True)
    return (center * lax.rsqrt(spread + EPSILON)).reshape(field_shape)


def gather_channels(field):
    return lax.all_gather(field, "mp", axis=1, tiled=True)


def pair_gather_channels(field):
    across = lax.ppermute(field, "mp", [(i, i ^ 2) for i in range(4)])
    beside = lax.ppermute(field, "mp", [(i, i ^ 1) for i in range(4)])
    relayed = lax.ppermute(across, "mp", [(i, i ^ 1) for i in range(4)])
    return jnp.concatenate([field, beside, across, relayed], axis=1)


def shift_parts(shard, count):
    parts = [shard]
    for step in range(1, count):
        parts.append(lax.ppermute(shard, "dp", [(i, (i + step) % count) for i in range(count)]))
    return jnp.stack(parts)


def order_rows(stacked, wanted_blocks):
    my_shard = lax.axis_index("dp")
    count = stacked.shape[0]
    picked = jnp.take(stacked, (my_shard - wanted_blocks) % count, axis=0, mode="clip")
    return picked.reshape((count * stacked.shape[1],) + stacked.shape[2:])


def gather_kernel(weight_shard):
    return lax.all_gather(weight_shard, "dp", axis=0, tiled=True)


def gather_projection(weight_shard):
    return lax.all_gather(weight_shard, "dp", axis=0, tiled=True)


def apply_kernel(full_field, kernel):
    sample_count = full_field.shape[0]
    out_width = kernel.shape[2]
    tap_images = jnp.einsum("scq,cte->steq", full_field, kernel, preferred_element_type=jnp.float32)
    tap_images = tap_images.reshape(sample_count, 9, out_width, SIDE, SIDE)
    padded = jnp.pad(tap_images, ((0, 0), (0, 0), (0, 0), (1, 1), (1, 1)))
    running = padded[:, 0, :, 0:SIDE, 0:SIDE]
    for offset in range(1, 9):
        row_shift, col_shift = (offset // 3, offset % 3)
        running = (
            running
            + padded[:, offset, :, row_shift : row_shift + SIDE, col_shift : col_shift + SIDE]
        )
    return running.reshape(sample_count, out_width, SIDE * SIDE)


def local(
    latents,
    modulation,
    first_kernel,
    second_kernel,
    encoder_cache,
    query_weight,
    output_weight,
    kept_prompt_list,
    destination,
    lengths,
):
    group_width = C // GROUPS
    dp_count = lax.axis_size("dp")
    mp_count = lax.axis_size("mp")
    my_shard = lax.axis_index("dp")
    my_column = lax.axis_index("mp")
    sample_shard_count = latents.shape[0]
    prompt_dev = encoder_cache.shape[0]
    cache_len = encoder_cache.shape[2]
    cache_width = encoder_cache.shape[1]
    cell_count = latents.shape[2]
    slot_limit = 2 * (sample_shard_count // dp_count)
    all_samples = destination.shape[0]
    owner_target = destination.reshape(dp_count, sample_shard_count)
    positions = jnp.arange(sample_shard_count, dtype=jnp.int32)
    before = positions[None, :] < positions[:, None]
    same_target = owner_target[:, :, None] == owner_target[:, None, :]
    slot_rank = jnp.sum((same_target & before[None]).astype(jnp.int32), axis=2)
    my_target = lax.dynamic_index_in_dim(owner_target, my_shard, 0, keepdims=False)
    my_rank = lax.dynamic_index_in_dim(slot_rank, my_shard, 0, keepdims=False)
    my_prompts = (
        lax.dynamic_slice_in_dim(
            kept_prompt_list, my_shard * sample_shard_count, sample_shard_count
        )
        - my_shard * prompt_dev
    )
    send_slot = my_target * slot_limit + my_rank
    slot_table = send_slot[:, None] == jnp.arange(dp_count * slot_limit, dtype=jnp.int32)[None, :]
    source_row = jnp.sum(jnp.where(slot_table, my_prompts[:, None], 0), axis=0)
    filled = jnp.any(slot_table, axis=0)
    send_rows = jnp.take(encoder_cache, source_row, axis=0)
    send_rows = jnp.where(filled[:, None, None], send_rows, jnp.zeros_like(send_rows))
    outgoing = send_rows.reshape(dp_count, slot_limit, cache_width, cache_len)
    incoming = lax.all_to_all(outgoing, "dp", split_axis=0, concat_axis=0, tiled=True)
    arriving = destination == my_shard
    arrival_pos = jnp.cumsum(arriving.astype(jnp.int32)) - 1
    selector = arriving[None, :] & (arrival_pos[None, :] == positions[:, None])
    kept_prompt = jnp.sum(
        jnp.where(selector, jnp.arange(all_samples, dtype=jnp.int32)[None, :], 0), axis=1
    )
    incoming_order_rank = jnp.sum(jnp.where(selector, slot_rank.reshape(-1)[None, :], 0), axis=1)
    prompt_ids = jnp.sum(jnp.where(selector, kept_prompt_list[None, :], 0), axis=1)
    landing_slot = kept_prompt // sample_shard_count * slot_limit + incoming_order_rank
    my_pairs = jnp.take(
        incoming.reshape(dp_count * slot_limit, cache_width, cache_len), landing_slot, axis=0
    )
    prompt_hits = prompt_ids[:, None] == jnp.arange(lengths.shape[0], dtype=jnp.int32)[None, :]
    my_lengths = jnp.sum(jnp.where(prompt_hits, lengths[None, :], 0), axis=1)
    fast = dp_count == 4 and mp_count == 4
    weight_shards = (first_kernel, second_kernel, query_weight, output_weight)
    if fast:
        block_ids = jnp.arange(dp_count, dtype=jnp.int32)
        channel_blocks = jnp.bitwise_xor(block_ids, my_column)
        full_weights = (
            order_rows(shift_parts(first_kernel, dp_count), channel_blocks),
            order_rows(shift_parts(second_kernel, dp_count), channel_blocks),
            order_rows(shift_parts(query_weight, dp_count), block_ids),
            order_rows(shift_parts(output_weight, dp_count), block_ids),
        )
        spread_channels = pair_gather_channels
    else:
        full_weights = (
            gather_kernel(first_kernel),
            gather_kernel(second_kernel),
            gather_projection(query_weight),
            gather_projection(output_weight),
        )
        spread_channels = gather_channels
    start_field = latents.astype(jnp.float32)
    activated = jax.nn.silu(norm_groups(start_field, group_width)).astype(jnp.bfloat16)
    first_in = spread_channels(activated)

    def convolve(full_field, which_weight):
        return apply_kernel(full_field, full_weights[which_weight])

    def project(field_rows, which_weight):
        full_weight = full_weights[which_weight]
        return jnp.einsum(
            "scq,ce->seq", field_rows, full_weight, preferred_element_type=jnp.float32
        )

    first_out = convolve(first_in, 0)
    scale_term = modulation[:, 0, :].astype(jnp.float32)[:, :, None]
    shift_term = modulation[:, 1, :].astype(jnp.float32)[:, :, None]
    modulated = jax.nn.silu(
        norm_groups(first_out, group_width) * (1.0 + scale_term) + shift_term
    ).astype(jnp.bfloat16)
    second_in = spread_channels(modulated)
    residual = start_field + convolve(second_in, 1)
    normed_out = norm_groups(residual, group_width).astype(jnp.bfloat16)
    local_samples = sample_shard_count // mp_count
    query_cells, pair_heads = (
        lax.all_to_all(normed_out, "mp", split_axis=0, concat_axis=1, tiled=True),
        lax.all_to_all(my_pairs, "mp", split_axis=0, concat_axis=1, tiled=True),
    )
    total_width = query_cells.shape[1]
    head_count = total_width // HEAD
    queries = project(query_cells, 2).astype(jnp.bfloat16)
    queries = queries.reshape(local_samples, head_count, HEAD, cell_count)
    heads_of_keys = pair_heads[:, :total_width, :].reshape(
        local_samples, head_count, HEAD, cache_len
    )
    value_heads = pair_heads[:, total_width:, :].reshape(local_samples, head_count, HEAD, cache_len)
    scores = jnp.einsum(
        "shdq,shdk->shqk", queries, heads_of_keys, preferred_element_type=jnp.float32
    ) * HEAD ** (-0.5)
    local_lengths = lax.dynamic_slice_in_dim(my_lengths, my_column * local_samples, local_samples)
    visible = (
        jnp.arange(cache_len, dtype=jnp.int32)[None, None, None, :]
        < local_lengths[:, None, None, None]
    )
    scores = jnp.where(visible, scores, MASKED)
    row_peak = jnp.max(scores, axis=3, keepdims=True)
    exponent = jnp.exp(scores - row_peak)
    attention = (exponent / jnp.sum(exponent, axis=3, keepdims=True)).astype(jnp.bfloat16)
    context = jnp.einsum(
        "shqk,shdk->shdq", attention, value_heads, preferred_element_type=jnp.float32
    ).astype(jnp.bfloat16)
    attended = project(context.reshape(local_samples, total_width, cell_count), 3).astype(
        jnp.bfloat16
    )
    returned = lax.all_to_all(attended, "mp", split_axis=1, concat_axis=0, tiled=True)
    final_field = residual + returned.astype(jnp.float32)
    return final_field.astype(jnp.bfloat16)


def solution(mesh):
    in_specs = (
        P(("groups", "dp"), "mp", None),
        P(("groups", "dp"), None, "mp"),
        P("dp", None, "mp"),
        P("dp", None, "mp"),
        P(("groups", "dp"), "mp", None),
        P("dp", None),
        P("dp", None),
        P("groups"),
        P("groups"),
        P("groups"),
    )
    out_specs = P(("groups", "dp"), "mp", None)
    return jax.shard_map(local, mesh=mesh, in_specs=in_specs, out_specs=out_specs, check_vma=False)
```

profile of v0, /device:TPU:8, one launch (start us, length us, event | category | flops | bytes accessed | tf_op | source)
XLA Modules:
  0.0 435.4 jit_solution(7232761819546583479)
XLA Ops:
  2.3 3.5 gather_fusion.3
  5.8 5.5 %select_select_fusion = bf16[4,16,320,128]{3,2,1,0:T(8,128)(2,1)} fusion(bf16[4,16,320,128]{3,2,1,0:T(8,128)(2,1)} %bitcast.138, pred[4,16]{1,0:T(4,128)(4,1)S(1)} %compare_and_fusion, pred[4,16]{1,0:T(4,128)(4,1)S(1)} %broadcast_in_dim.133), kind=kLoop, calls=%fused_computation.25 | loop fusion | flops 5242880 | bytes 10485888 | tf_op jit(solution)/shard_map/jit(_where)/select_n | solution.py:115
  11.3 5.4 %all-to-all-start = ((bf16[4,16,320,128]{3,2,1,0:T(8,128)(2,1)}), bf16[4,16,320,128]{3,2,1,0:T(8,128)(2,1)}, u32[]{:S(2)}, u32[]{:S(2)}) async-start(bf16[4,16,320,128]{3,2,1,0:T(8,128)(2,1)} %select_select_fusion), calls=%async_computation | async-start | bytes 10485760 | tf_op jit(solution)/shard_map/all_to_all | solution.py:117
  23.9 2.0 collective-permute-start.5
  26.0 18.9 %collective-permute-done.7 = bf16[32,160,64]{1,2,0:T(8,128)(2,1)} collective-permute-done((bf16[32,160,64]{1,2,0:T(8,128)(2,1)}, bf16[32,160,64]{1,2,0:T(8,128)(2,1)}, u32[]{:S(2)}, u32[]{:S(2)}) %collective-permute-start.7) | collective-permute-done | bytes 655392 | tf_op jit(solution)/shard_map/ppermute | solution.py:29
  44.9 132.9 %collective-permute-done.3 = bf16[160,9,160]{2,0,1:T(8,128)(2,1)S(1)} collective-permute-done((bf16[160,9,160]{2,0,1:T(8,128)(2,1)S(1)}, bf16[160,9,160]{2,0,1:T(8,128)(2,1)S(1)}, u32[]{:S(2)}, u32[]{:S(2)}) %collective-permute-start.3) | collective-permute-done | bytes 460832 | tf_op jit(solution)/shard_map/ppermute | solution.py:38
  177.9 14.6 %collective-permute-done.4 = bf16[160,9,160]{2,0,1:T(8,128)(2,1)S(1)} collective-permute-done((bf16[160,9,160]{2,0,1:T(8,128)(2,1)S(1)}, bf16[160,9,160]{2,0,1:T(8,128)(2,1)S(1)}, u32[]{:S(2)}, u32[]{:S(2)}) %collective-permute-start.4) | collective-permute-done | bytes 460832 | tf_op jit(solution)/shard_map/ppermute | solution.py:38
  192.5 2.0 collective-permute-done.5
  195.4 2.2 pad_maximum_fusion.1
  197.6 2.4 gather_fusion.1
  200.0 6.2 %copy.50 = bf16[4,160,9,160]{1,0,3,2:T(4,128)(2,1)S(1)} copy(bf16[4,160,9,160]{3,1,2,0:T(8,128)(2,1)} %gather_fusion.1) | data formatting | bytes 3686400 | tf_op jit(solution)/shard_map/jit(_take)/gather | solution.py:45
  206.2 3.0 reshape.482
  209.2 11.4 %convolution_bitcast_fusion.1 = f32[32,9,160,8,8]{2,4,3,0,1:T(8,128)S(1)} fusion(bf16[32,160,64]{1,2,0:T(8,128)(2,1)} %collective-permute-done.8, bf16[32,160,64]{1,2,0:T(8,128)(2,1)} %collective-permute-done.7, bf16[32,160,64]{1,2,0:T(8,128)(2,1)} %collective-permute-done.6, bf16[32,160,64]{1,2,0:T(8,128)(2,1)} %fusion.36, ...), kind=kOutput, calls=%fused_computation.24 | convolution fusion | flops 3785359360 | bytes 16261120 | tf_op jit(solution)/shard_map/scq,cte->steq/dot_general | solution.py:60
  220.6 2.3 fusion.75
  224.1 1.7 multiply_convert_fusion.1
  229.1 2.0 collective-permute-start.2
  231.5 18.9 %collective-permute-done.10 = bf16[32,160,64]{1,2,0:T(8,128)(2,1)} collective-permute-done((bf16[32,160,64]{1,2,0:T(8,128)(2,1)}, bf16[32,160,64]{1,2,0:T(8,128)(2,1)}, u32[]{:S(2)}, u32[]{:S(2)}) %collective-permute-start.10) | collective-permute-done | bytes 655392 | tf_op jit(solution)/shard_map/ppermute | solution.py:29
  250.7 25.1 %collective-permute-done = bf16[160,9,160]{2,0,1:T(8,128)(2,1)S(1)} collective-permute-done((bf16[160,9,160]{2,0,1:T(8,128)(2,1)S(1)}, bf16[160,9,160]{2,0,1:T(8,128)(2,1)S(1)}, u32[]{:S(2)}, u32[]{:S(2)}) %collective-permute-start) | collective-permute-done | bytes 460832 | tf_op jit(solution)/shard_map/ppermute | solution.py:38
  275.8 13.9 %collective-permute-done.1 = bf16[160,9,160]{2,0,1:T(8,128)(2,1)S(1)} collective-permute-done((bf16[160,9,160]{2,0,1:T(8,128)(2,1)S(1)}, bf16[160,9,160]{2,0,1:T(8,128)(2,1)S(1)}, u32[]{:S(2)}, u32[]{:S(2)}) %collective-permute-start.1) | collective-permute-done | bytes 460832 | tf_op jit(solution)/shard_map/ppermute | solution.py:38
  289.7 2.2 collective-permute-done.2
  292.0 2.2 pad_maximum_fusion
  294.1 2.4 gather_fusion
  296.6 6.2 %copy.49 = bf16[4,160,9,160]{1,0,3,2:T(4,128)(2,1)S(1)} copy(bf16[4,160,9,160]{3,1,2,0:T(8,128)(2,1)} %gather_fusion) | data formatting | bytes 3686400 | tf_op jit(solution)/shard_map/jit(_take)/gather | solution.py:45
  302.8 3.0 reshape.484
  305.7 11.5 %convolution_bitcast_fusion = f32[32,9,160,8,8]{2,4,3,0,1:T(8,128)S(1)} fusion(bf16[32,160,64]{1,2,0:T(8,128)(2,1)} %collective-permute-done.11, bf16[32,160,64]{1,2,0:T(8,128)(2,1)} %collective-permute-done.10, bf16[32,160,64]{1,2,0:T(8,128)(2,1)} %collective-permute-done.9, bf16[32,160,64]{1,2,0:T(8,128)(2,1)} %multiply_convert_fusion.1, ...), kind=kOutput, calls=%fused_computation.23 | convolution fusion | flops 3785359360 | bytes 16261120 | tf_op jit(solution)/shard_map/scq,cte->steq/dot_general | solution.py:60
  317.2 2.4 fusion.74
  322.2 4.3 all-to-all-start.2
  326.5 3.5 gather_fusion.4
  330.1 1.8 broadcast_select_fusion
  331.9 9.1 %all-to-all-done.2 = bf16[32,160,64]{1,2,0:T(8,128)(2,1)} async-done(((bf16[32,160,64]{1,2,0:T(8,128)(2,1)}), bf16[32,160,64]{1,2,0:T(8,128)(2,1)}, u32[]{:S(2)}, u32[]{:S(2)}) %all-to-all-start.2) | async-done | bytes 655392 | tf_op jit(solution)/shard_map/all_to_all | solution.py:176
  341.0 3.7 all-to-all-start.1
  344.7 2.0 collective-permute-start.16
  346.8 1.9 collective-permute-start.17
  348.8 2.7 collective-permute-start.13
  354.3 9.2 %collective-permute-done.16 = bf16[160,640]{1,0:T(8,128)(2,1)S(1)} collective-permute-done((bf16[160,640]{1,0:T(8,128)(2,1)S(1)}, bf16[160,640]{1,0:T(8,128)(2,1)S(1)}, u32[]{:S(2)}, u32[]{:S(2)}) %collective-permute-start.16) | collective-permute-done | bytes 204832 | tf_op jit(solution)/shard_map/ppermute | solution.py:38
  363.4 11.0 %collective-permute-done.17 = bf16[160,640]{1,0:T(8,128)(2,1)S(1)} collective-permute-done((bf16[160,640]{1,0:T(8,128)(2,1)S(1)}, bf16[160,640]{1,0:T(8,128)(2,1)S(1)}, u32[]{:S(2)}, u32[]{:S(2)}) %collective-permute-start.17) | collective-permute-done | bytes 204832 | tf_op jit(solution)/shard_map/ppermute | solution.py:38
  378.0 2.8 collective-permute-done.13
  380.8 2.5 collective-permute-done.14
  383.3 2.2 pad_maximum_fusion.3
  385.5 1.8 gather_fusion.2
  387.4 3.1 fusion.50
  390.5 2.3 copy.56
  394.7 2.1 fusion.80
  396.8 1.9 fusion.79
  398.7 11.1 %convolution_convert_fusion = bf16[8,10,64,64]{3,2,1,0:T(8,128)(2,1)S(1)} fusion(bf16[8,10,64,128]{3,2,1,0:T(8,128)(2,1)} %bitcast.150, f32[8,10,64]{2,1,0:T(8,128)S(1)} %fusion.79, f32[8,10,64,128]{3,2,1,0:T(8,128)} %fusion.80, pred[8,128]{1,0:T(8,128)(4,1)S(1)} %iota_compare_fusion.4), kind=kOutput, calls=%fused_computation.87 | convolution fusion | flops 87495808 | bytes 4609024 | tf_op jit(solution)/shard_map/shqk,shdk->shdq/dot_general | solution.py:199
  413.7 13.0 %all_to_all.47 = bf16[4,2,40960]{2,1,0:T(2,128)(2,1)S(1)} all-to-all(bf16[4,2,40960]{2,1,0:T(2,128)(2,1)S(1)} %reshape.493), channel_id=1, replica_groups=mesh['groups'=2,'dp'=4,'mp'=4] {'mp'}, dimensions={0} | all-to-all | bytes 1310720 | tf_op jit(solution)/shard_map/all_to_all | solution.py:205
  428.4 3.5 copy.60
  431.9 3.5 fusion.38
  (140 shorter events, 31.7 us)
Async XLA Ops:
  0.0 2.3 copy-start
  11.3 5.5 %copy-start.3 = (bf16[32,160,64]{1,2,0:T(8,128)(2,1)S(1)}, bf16[32,160,64]{1,2,0:T(8,128)(2,1)}, u32[]{:S(2)}) copy-start(bf16[32,160,64]{1,2,0:T(8,128)(2,1)} %param.10) | copy-start | bytes 1966084
  11.3 310.9 %all-to-all-start = ((bf16[4,16,320,128]{3,2,1,0:T(8,128)(2,1)}), bf16[4,16,320,128]{3,2,1,0:T(8,128)(2,1)}, u32[]{:S(2)}, u32[]{:S(2)}) async-start(bf16[4,16,320,128]{3,2,1,0:T(8,128)(2,1)} %select_select_fusion), calls=%async_computation | async-start | bytes 10485760 | tf_op jit(solution)/shard_map/all_to_all | solution.py:117
  17.3 4.3 copy-start.6
  17.3 8.7 %copy-start.17 = (bf16[32,2,160]{2,1,0:T(2,128)(2,1)S(1)}, bf16[32,2,160]{2,1,0:T(2,128)(2,1)}, u32[]{:S(2)}) copy-start(bf16[32,2,160]{2,1,0:T(2,128)(2,1)} %param.11) | copy-start | bytes 61444
  19.9 25.0 %collective-permute-start.7 = (bf16[32,160,64]{1,2,0:T(8,128)(2,1)}, bf16[32,160,64]{1,2,0:T(8,128)(2,1)}, u32[]{:S(2)}, u32[]{:S(2)}) collective-permute-start(bf16[32,160,64]{1,2,0:T(8,128)(2,1)} %fusion.36), channel_id=1, source_target_pairs={{0,2},{1,3},{2,0},{3,1},{4,6},{5,7},{6,4},{7,5},{8,10},{9,11},{10,... | collective-permute-start | bytes 1966088 | tf_op jit(solution)/shard_map/ppermute | solution.py:29
  21.5 156.3 %collective-permute-start.3 = (bf16[160,9,160]{2,0,1:T(8,128)(2,1)S(1)}, bf16[160,9,160]{2,0,1:T(8,128)(2,1)S(1)}, u32[]{:S(2)}, u32[]{:S(2)}) collective-permute-start(bf16[160,9,160]{2,0,1:T(8,128)(2,1)S(1)} %copy-done.6), channel_id=1, source_target_pairs={{0,4},{4,8},{8,12},{12,0},{1,5},{5,9},{9,13},{13,1},{2,6},{6,10},{... | collective-permute-start | bytes 1382408 | tf_op jit(solution)/shard_map/ppermute | solution.py:38
  23.0 169.5 %collective-permute-start.4 = (bf16[160,9,160]{2,0,1:T(8,128)(2,1)S(1)}, bf16[160,9,160]{2,0,1:T(8,128)(2,1)S(1)}, u32[]{:S(2)}, u32[]{:S(2)}) collective-permute-start(bf16[160,9,160]{2,0,1:T(8,128)(2,1)S(1)} %copy-done.6), channel_id=1, source_target_pairs={{0,8},{4,12},{8,0},{12,4},{1,9},{5,13},{9,1},{13,5},{2,10},{6,14},... | collective-permute-start | bytes 1382408 | tf_op jit(solution)/shard_map/ppermute | solution.py:38
  23.9 170.6 %collective-permute-start.5 = (bf16[160,9,160]{2,0,1:T(8,128)(2,1)S(1)}, bf16[160,9,160]{2,0,1:T(8,128)(2,1)S(1)}, u32[]{:S(2)}, u32[]{:S(2)}) collective-permute-start(bf16[160,9,160]{2,0,1:T(8,128)(2,1)S(1)} %copy-done.6), channel_id=1, source_target_pairs={{0,12},{4,0},{8,4},{12,8},{1,13},{5,1},{9,5},{13,9},{2,14},{6,2},{... | collective-permute-start | bytes 1382408 | tf_op jit(solution)/shard_map/ppermute | solution.py:38
  25.9 183.3 %collective-permute-start.6 = (bf16[32,160,64]{1,2,0:T(8,128)(2,1)}, bf16[32,160,64]{1,2,0:T(8,128)(2,1)}, u32[]{:S(2)}, u32[]{:S(2)}) collective-permute-start(bf16[32,160,64]{1,2,0:T(8,128)(2,1)} %fusion.36), channel_id=1, source_target_pairs={{0,1},{1,0},{2,3},{3,2},{4,5},{5,4},{6,7},{7,6},{8,9},{9,8},{10,11... | collective-permute-start | bytes 1966088 | tf_op jit(solution)/shard_map/ppermute | solution.py:30
  44.9 164.3 %collective-permute-start.8 = (bf16[32,160,64]{1,2,0:T(8,128)(2,1)}, bf16[32,160,64]{1,2,0:T(8,128)(2,1)}, u32[]{:S(2)}, u32[]{:S(2)}) collective-permute-start(bf16[32,160,64]{1,2,0:T(8,128)(2,1)} %collective-permute-done.7), channel_id=1, source_target_pairs={{0,1},{1,0},{2,3},{3,2},{4,5},{5,4},{6,7},{7,6},{8,9},{9,8},{10,11... | collective-permute-start | bytes 1966088 | tf_op jit(solution)/shard_map/ppermute | solution.py:31
  177.8 16.7 %copy-start.10 = (bf16[160,9,160]{2,0,1:T(8,128)(2,1)}, bf16[160,9,160]{2,0,1:T(8,128)(2,1)S(1)}, u32[]{:S(2)}) copy-start(bf16[160,9,160]{2,0,1:T(8,128)(2,1)S(1)} %collective-permute-done.3) | copy-start | bytes 1382404
  192.5 2.1 copy-start.11
  194.5 0.9 copy-start.12
  223.7 3.7 copy-start.7
  223.7 7.4 %copy-start.18 = (s32[128]{0:T(128)S(1)}, s32[128]{0:T(128)}, u32[]{:S(2)}) copy-start(s32[128]{0:T(128)} %param.18) | copy-start | bytes 1540
  223.7 26.9 %copy-start.19 = (s32[128]{0:T(128)S(1)}, s32[128]{0:T(128)}, u32[]{:S(2)}) copy-start(s32[128]{0:T(128)} %param.17) | copy-start | bytes 1540
  225.9 24.5 %collective-permute-start.10 = (bf16[32,160,64]{1,2,0:T(8,128)(2,1)}, bf16[32,160,64]{1,2,0:T(8,128)(2,1)}, u32[]{:S(2)}, u32[]{:S(2)}) collective-permute-start(bf16[32,160,64]{1,2,0:T(8,128)(2,1)} %multiply_convert_fusion.1), channel_id=1, source_target_pairs={{0,2},{1,3},{2,0},{3,1},{4,6},{5,7},{6,4},{7,5},{8,10},{9,11},{10,... | collective-permute-start | bytes 1966088 | tf_op jit(solution)/shard_map/ppermute | solution.py:29
  227.4 48.4 %collective-permute-start = (bf16[160,9,160]{2,0,1:T(8,128)(2,1)S(1)}, bf16[160,9,160]{2,0,1:T(8,128)(2,1)S(1)}, u32[]{:S(2)}, u32[]{:S(2)}) collective-permute-start(bf16[160,9,160]{2,0,1:T(8,128)(2,1)S(1)} %copy-done.7), channel_id=1, source_target_pairs={{0,4},{4,8},{8,12},{12,0},{1,5},{5,9},{9,13},{13,1},{2,6},{6,10},{... | collective-permute-start | bytes 1382408 | tf_op jit(solution)/shard_map/ppermute | solution.py:38
  227.4 62.3 %collective-permute-start.1 = (bf16[160,9,160]{2,0,1:T(8,128)(2,1)S(1)}, bf16[160,9,160]{2,0,1:T(8,128)(2,1)S(1)}, u32[]{:S(2)}, u32[]{:S(2)}) collective-permute-start(bf16[160,9,160]{2,0,1:T(8,128)(2,1)S(1)} %copy-done.7), channel_id=1, source_target_pairs={{0,8},{4,12},{8,0},{12,4},{1,9},{5,13},{9,1},{13,5},{2,10},{6,14},... | collective-permute-start | bytes 1382408 | tf_op jit(solution)/shard_map/ppermute | solution.py:38
  229.1 62.9 %collective-permute-start.2 = (bf16[160,9,160]{2,0,1:T(8,128)(2,1)S(1)}, bf16[160,9,160]{2,0,1:T(8,128)(2,1)}, u32[]{:S(2)}, u32[]{:S(2)}) collective-permute-start(bf16[160,9,160]{2,0,1:T(8,128)(2,1)S(1)} %copy-done.7), channel_id=1, source_target_pairs={{0,12},{4,0},{8,4},{12,8},{1,13},{5,1},{9,5},{13,9},{2,14},{6,2},{... | collective-permute-start | bytes 1382408 | tf_op jit(solution)/shard_map/ppermute | solution.py:38
  231.4 74.4 %collective-permute-start.9 = (bf16[32,160,64]{1,2,0:T(8,128)(2,1)}, bf16[32,160,64]{1,2,0:T(8,128)(2,1)}, u32[]{:S(2)}, u32[]{:S(2)}) collective-permute-start(bf16[32,160,64]{1,2,0:T(8,128)(2,1)} %multiply_convert_fusion.1), channel_id=1, source_target_pairs={{0,1},{1,0},{2,3},{3,2},{4,5},{5,4},{6,7},{7,6},{8,9},{9,8},{10,11... | collective-permute-start | bytes 1966088 | tf_op jit(solution)/shard_map/ppermute | solution.py:30
  250.4 55.4 %collective-permute-start.11 = (bf16[32,160,64]{1,2,0:T(8,128)(2,1)}, bf16[32,160,64]{1,2,0:T(8,128)(2,1)}, u32[]{:S(2)}, u32[]{:S(2)}) collective-permute-start(bf16[32,160,64]{1,2,0:T(8,128)(2,1)} %collective-permute-done.10), channel_id=1, source_target_pairs={{0,1},{1,0},{2,3},{3,2},{4,5},{5,4},{6,7},{7,6},{8,9},{9,8},{10,11... | collective-permute-start | bytes 1966088 | tf_op jit(solution)/shard_map/ppermute | solution.py:31
  275.8 16.2 %copy-start.8 = (bf16[160,9,160]{2,0,1:T(8,128)(2,1)}, bf16[160,9,160]{2,0,1:T(8,128)(2,1)S(1)}, u32[]{:S(2)}) copy-start(bf16[160,9,160]{2,0,1:T(8,128)(2,1)S(1)} %collective-permute-done) | copy-start | bytes 1382404
  289.7 2.2 copy-start.9
  305.7 11.5 %copy-start.4 = (bf16[32,160,64]{1,2,0:T(8,128)(2,1)S(1)}, bf16[32,160,64]{1,2,0:T(8,128)(2,1)}, u32[]{:S(2)}) copy-start(bf16[32,160,64]{1,2,0:T(8,128)(2,1)} %param.10) | copy-start | bytes 1966084
  319.7 2.6 copy-start.2
  322.2 18.8 %all-to-all-start.2 = ((bf16[32,160,64]{1,2,0:T(8,128)(2,1)}), bf16[32,160,64]{1,2,0:T(8,128)(2,1)}, u32[]{:S(2)}, u32[]{:S(2)}) async-start(bf16[32,160,64]{1,2,0:T(8,128)(2,1)} %multiply_convert_fusion), calls=%async_computation.2 | async-start | bytes 2097152 | tf_op jit(solution)/shard_map/all_to_all | solution.py:176
  331.9 12.8 %copy-start.13 = (bf16[160,640]{1,0:T(8,128)(2,1)S(1)}, bf16[160,640]{1,0:T(8,128)(2,1)}, u32[]{:S(2)}) copy-start(bf16[160,640]{1,0:T(8,128)(2,1)} %param.15) | copy-start | bytes 614404
  331.9 19.7 %copy-start.20 = (s32[168]{0:T(256)S(1)}, s32[168]{0:T(256)}, u32[]{:S(2)}) copy-start(s32[168]{0:T(256)} %param.19) | copy-start | bytes 2020
  341.0 51.8 %all-to-all-start.1 = ((bf16[32,320,128]{2,1,0:T(8,128)(2,1)}), bf16[32,320,128]{2,1,0:T(8,128)(2,1)S(1)}, u32[]{:S(2)}, u32[]{:S(2)}) async-start(bf16[32,320,128]{2,1,0:T(8,128)(2,1)} %broadcast_select_fusion), calls=%async_computation.1 | async-start | bytes 5242880 | tf_op jit(solution)/shard_map/all_to_all | solution.py:177
  344.7 7.9 %collective-permute-start.15 = (bf16[160,640]{1,0:T(8,128)(2,1)S(1)}, bf16[160,640]{1,0:T(8,128)(2,1)S(1)}, u32[]{:S(2)}, u32[]{:S(2)}) collective-permute-start(bf16[160,640]{1,0:T(8,128)(2,1)S(1)} %copy-done.13), channel_id=1, source_target_pairs={{0,4},{4,8},{8,12},{12,0},{1,5},{5,9},{9,13},{13,1},{2,6},{6,10},{... | collective-permute-start | bytes 614408 | tf_op jit(solution)/shard_map/ppermute | solution.py:38
  344.7 18.7 %collective-permute-start.16 = (bf16[160,640]{1,0:T(8,128)(2,1)S(1)}, bf16[160,640]{1,0:T(8,128)(2,1)S(1)}, u32[]{:S(2)}, u32[]{:S(2)}) collective-permute-start(bf16[160,640]{1,0:T(8,128)(2,1)S(1)} %copy-done.13), channel_id=1, source_target_pairs={{0,8},{4,12},{8,0},{12,4},{1,9},{5,13},{9,1},{13,5},{2,10},{6,14},... | collective-permute-start | bytes 614408 | tf_op jit(solution)/shard_map/ppermute | solution.py:38
  346.8 27.7 %collective-permute-start.17 = (bf16[160,640]{1,0:T(8,128)(2,1)S(1)}, bf16[160,640]{1,0:T(8,128)(2,1)S(1)}, u32[]{:S(2)}, u32[]{:S(2)}) collective-permute-start(bf16[160,640]{1,0:T(8,128)(2,1)S(1)} %copy-done.13), channel_id=1, source_target_pairs={{0,12},{4,0},{8,4},{12,8},{1,13},{5,1},{9,5},{13,9},{2,14},{6,2},{... | collective-permute-start | bytes 614408 | tf_op jit(solution)/shard_map/ppermute | solution.py:38
  348.7 29.3 %collective-permute-start.12 = (bf16[160,640]{1,0:T(8,128)(2,1)}, bf16[160,640]{1,0:T(8,128)(2,1)}, u32[]{:S(2)}, u32[]{:S(2)}) collective-permute-start(bf16[160,640]{1,0:T(8,128)(2,1)} %param.16), channel_id=1, source_target_pairs={{0,4},{4,8},{8,12},{12,0},{1,5},{5,9},{9,13},{13,1},{2,6},{6,10},{... | collective-permute-start | bytes 614408 | tf_op jit(solution)/shard_map/ppermute | solution.py:38
  348.8 32.0 %collective-permute-start.13 = (bf16[160,640]{1,0:T(8,128)(2,1)}, bf16[160,640]{1,0:T(8,128)(2,1)}, u32[]{:S(2)}, u32[]{:S(2)}) collective-permute-start(bf16[160,640]{1,0:T(8,128)(2,1)} %param.16), channel_id=1, source_target_pairs={{0,8},{4,12},{8,0},{12,4},{1,9},{5,13},{9,1},{13,5},{2,10},{6,14},... | collective-permute-start | bytes 614408 | tf_op jit(solution)/shard_map/ppermute | solution.py:38
  352.6 21.9 %copy-start.14 = (bf16[160,640]{1,0:T(8,128)(2,1)}, bf16[160,640]{1,0:T(8,128)(2,1)S(1)}, u32[]{:S(2)}) copy-start(bf16[160,640]{1,0:T(8,128)(2,1)S(1)} %collective-permute-done.15) | copy-start | bytes 614404
  352.6 30.7 %collective-permute-start.14 = (bf16[160,640]{1,0:T(8,128)(2,1)}, bf16[160,640]{1,0:T(8,128)(2,1)}, u32[]{:S(2)}, u32[]{:S(2)}) collective-permute-start(bf16[160,640]{1,0:T(8,128)(2,1)} %param.16), channel_id=1, source_target_pairs={{0,12},{4,0},{8,4},{12,8},{1,13},{5,1},{9,5},{13,9},{2,14},{6,2},{... | collective-permute-start | bytes 614408 | tf_op jit(solution)/shard_map/ppermute | solution.py:38
  363.4 11.1 %copy-start.15 = (bf16[160,640]{1,0:T(8,128)(2,1)}, bf16[160,640]{1,0:T(8,128)(2,1)S(1)}, u32[]{:S(2)}) copy-start(bf16[160,640]{1,0:T(8,128)(2,1)S(1)} %collective-permute-done.16) | copy-start | bytes 614404
  374.5 0.7 copy-start.16
  393.0 1.7 copy-start.5
  428.4 7.1 %copy-start.1 = (bf16[42,320,128]{2,1,0:T(8,128)(2,1)S(1)}, bf16[42,320,128]{2,1,0:T(8,128)(2,1)}, u32[]{:S(2)}) copy-start(bf16[42,320,128]{2,1,0:T(8,128)(2,1)} %param.14) | copy-start | bytes 10321924
where the time goes:
time: 436 us; the launch traced here: 435 us
  waiting for transfers between devices  264 us (61%)
  local copies, waits for them, and re-layouts  50.8 us (12%)
  matrix products  41.8 us (10%)
  starting transfers between devices  33.2 us (8%)
  other arithmetic  32.2 us (7%)
  blocking collectives  13 us (3%)
    ppermute x12, waiting for transfers between devices, shift_parts(): lax.ppermute(shard, 'dp', [(i, (i + step) % count) for i in range(count)])  217 us
    ppermute x2, waiting for transfers between devices, pair_gather_channels(): across = lax.ppermute(field, 'mp', [(i, i ^ 2) for i in range(4)])  37.8 us
    dot_general x2, matrix products, apply_kernel(): jnp.einsum('scq,cte->steq', full_field, kernel, preferred_element_type=jn...  22.8 us
    gather x6, local copies, waits for them, and re-layouts, order_rows(): jnp.take(stacked, (my_shard - wanted_blocks) % count, axis=0, mode='clip')  20.6 us
    ppermute x12, starting transfers between devices, shift_parts(): lax.ppermute(shard, 'dp', [(i, (i + step) % count) for i in range(count)])  16.6 us
    all_to_all x1, blocking collectives, local(): lax.all_to_all(attended, 'mp', split_axis=1, concat_axis=0, tiled=True)  13 us
    dot_general x1, matrix products, local(): jnp.einsum('shqk,shdk->shdq', attention, value_heads, preferred_element_t...  11.1 us
    all_to_all x1, waiting for transfers between devices, local(): lax.all_to_all(normed_out, 'mp', split_axis=0, concat_axis=1, tiled=True)  9.13 us
  transfers between devices with their start and end apart: 21, of which 14 were waited for; matrix products, arithmetic and copies ran while one was open for 19% of the time, Pallas kernels for 0%

commit v1 on v0

--- a/solution.py
+++ b/solution.py
@@ -202,7 +202,10 @@
     attended = project(context.reshape(local_samples, total_width, cell_count), 3).astype(
         jnp.bfloat16
     )
-    returned = lax.all_to_all(attended, "mp", split_axis=1, concat_axis=0, tiled=True)
+    n_dev = lax.axis_size("mp")
+    blocks = jnp.stack(jnp.split(attended, n_dev, axis=1), axis=0)
+    blocks = lax.all_to_all(blocks, "mp", split_axis=0, concat_axis=0)
+    returned = jnp.concatenate(blocks, axis=0)
     final_field = residual + returned.astype(jnp.float32)
     return final_field.astype(jnp.bfloat16)
 

time: 436 us -> 432 us (level)
  local copies, waits for them, and re-layouts: 50.8 us -> 43.5 us
  blocking collectives: 13 us -> 17.5 us
    convert_element_type x2 -> x0, local copies, waits for them, and re-layouts: 4.87 us -> none  [the longest x1 3.53 us: local(): final_field = residual + returned.astype(jnp.float32)]
    all_to_all x1, blocking collectives: 13 us -> 17.5 us  [local(): blocks = lax.all_to_all(blocks, 'mp', split_axis=0, concat_axis=0)]
where the time goes in v1:
time: 432 us; the launch traced here: 431 us
  waiting for transfers between devices  264 us (61%)
  local copies, waits for them, and re-layouts  43.5 us (10%)
  matrix products  41.8 us (10%)
  starting transfers between devices  33.2 us (8%)
  other arithmetic  30.3 us (7%)
  blocking collectives  17.5 us (4%)
    ppermute x12, waiting for transfers between devices, shift_parts(): lax.ppermute(shard, 'dp', [(i, (i + step) % count) for i in range(count)])  217 us
    ppermute x2, waiting for transfers between devices, pair_gather_channels(): across = lax.ppermute(field, 'mp', [(i, i ^ 2) for i in range(4)])  37.8 us
    dot_general x2, matrix products, apply_kernel(): jnp.einsum('scq,cte->steq', full_field, kernel, preferred_element_type=jn...  22.8 us
    gather x6, local copies, waits for them, and re-layouts, order_rows(): jnp.take(stacked, (my_shard - wanted_blocks) % count, axis=0, mode='clip')  20.6 us
    all_to_all x1, blocking collectives, local(): blocks = lax.all_to_all(blocks, 'mp', split_axis=0, concat_axis=0)  17.5 us
    ppermute x12, starting transfers between devices, shift_parts(): lax.ppermute(shard, 'dp', [(i, (i + step) % count) for i in range(count)])  16.6 us
    dot_general x1, matrix products, local(): jnp.einsum('shqk,shdk->shdq', attention, value_heads, preferred_element_t...  11.1 us
    all_to_all x1, waiting for transfers between devices, local(): lax.all_to_all(normed_out, 'mp', split_axis=0, concat_axis=1, tiled=True)  9.13 us
  transfers between devices with their start and end apart: 21, of which 14 were waited for; matrix products, arithmetic and copies ran while one was open for 19% of the time, Pallas kernels for 0%

profile of v1, /device:TPU:8, one launch (start us, length us, event | category | flops | bytes accessed | tf_op | source)
XLA Modules:
  0.0 430.9 jit_solution(8085982260813021998)
XLA Ops:
  2.3 3.5 gather_fusion.3
  5.8 5.5 %select_select_fusion = bf16[4,16,320,128]{3,2,1,0:T(8,128)(2,1)} fusion(bf16[4,16,320,128]{3,2,1,0:T(8,128)(2,1)} %bitcast.139, pred[4,16]{1,0:T(4,128)(4,1)S(1)} %compare_and_fusion, pred[4,16]{1,0:T(4,128)(4,1)S(1)} %broadcast_in_dim.133), kind=kLoop, calls=%fused_computation.25 | loop fusion | flops 5242880 | bytes 10485888 | tf_op jit(solution)/shard_map/jit(_where)/select_n | solution.py:115
  11.3 5.4 %all-to-all-start = ((bf16[4,16,320,128]{3,2,1,0:T(8,128)(2,1)}), bf16[4,16,320,128]{3,2,1,0:T(8,128)(2,1)}, u32[]{:S(2)}, u32[]{:S(2)}) async-start(bf16[4,16,320,128]{3,2,1,0:T(8,128)(2,1)} %select_select_fusion), calls=%async_computation | async-start | bytes 10485760 | tf_op jit(solution)/shard_map/all_to_all | solution.py:117
  23.9 2.0 collective-permute-start.5
  26.0 18.9 %collective-permute-done.7 = bf16[32,160,64]{1,2,0:T(8,128)(2,1)} collective-permute-done((bf16[32,160,64]{1,2,0:T(8,128)(2,1)}, bf16[32,160,64]{1,2,0:T(8,128)(2,1)}, u32[]{:S(2)}, u32[]{:S(2)}) %collective-permute-start.7) | collective-permute-done | bytes 655392 | tf_op jit(solution)/shard_map/ppermute | solution.py:29
  44.9 132.9 %collective-permute-done.3 = bf16[160,9,160]{2,0,1:T(8,128)(2,1)S(1)} collective-permute-done((bf16[160,9,160]{2,0,1:T(8,128)(2,1)S(1)}, bf16[160,9,160]{2,0,1:T(8,128)(2,1)S(1)}, u32[]{:S(2)}, u32[]{:S(2)}) %collective-permute-start.3) | collective-permute-done | bytes 460832 | tf_op jit(solution)/shard_map/ppermute | solution.py:38
  177.9 14.6 %collective-permute-done.4 = bf16[160,9,160]{2,0,1:T(8,128)(2,1)S(1)} collective-permute-done((bf16[160,9,160]{2,0,1:T(8,128)(2,1)S(1)}, bf16[160,9,160]{2,0,1:T(8,128)(2,1)S(1)}, u32[]{:S(2)}, u32[]{:S(2)}) %collective-permute-start.4) | collective-permute-done | bytes 460832 | tf_op jit(solution)/shard_map/ppermute | solution.py:38
  192.5 2.0 collective-permute-done.5
  195.4 2.2 pad_maximum_fusion.1
  197.6 2.4 gather_fusion.1
  200.0 6.2 %copy.35 = bf16[4,160,9,160]{1,0,3,2:T(4,128)(2,1)S(1)} copy(bf16[4,160,9,160]{3,1,2,0:T(8,128)(2,1)} %gather_fusion.1) | data formatting | bytes 3686400 | tf_op jit(solution)/shard_map/jit(_take)/gather | solution.py:45
  206.2 3.0 reshape.480
  209.2 11.4 %convolution_bitcast_fusion.1 = f32[32,9,160,8,8]{2,4,3,0,1:T(8,128)S(1)} fusion(bf16[32,160,64]{1,2,0:T(8,128)(2,1)} %collective-permute-done.8, bf16[32,160,64]{1,2,0:T(8,128)(2,1)} %collective-permute-done.7, bf16[32,160,64]{1,2,0:T(8,128)(2,1)} %collective-permute-done.6, bf16[32,160,64]{1,2,0:T(8,128)(2,1)} %fusion.36, ...), kind=kOutput, calls=%fused_computation.24 | convolution fusion | flops 3785359360 | bytes 16261120 | tf_op jit(solution)/shard_map/scq,cte->steq/dot_general | solution.py:60
  220.6 2.3 fusion.75
  224.1 1.7 multiply_convert_fusion.1
  227.4 1.7 collective-permute-start.1
  229.1 2.0 collective-permute-start.2
  231.5 18.9 %collective-permute-done.10 = bf16[32,160,64]{1,2,0:T(8,128)(2,1)} collective-permute-done((bf16[32,160,64]{1,2,0:T(8,128)(2,1)}, bf16[32,160,64]{1,2,0:T(8,128)(2,1)}, u32[]{:S(2)}, u32[]{:S(2)}) %collective-permute-start.10) | collective-permute-done | bytes 655392 | tf_op jit(solution)/shard_map/ppermute | solution.py:29
  250.7 25.1 %collective-permute-done = bf16[160,9,160]{2,0,1:T(8,128)(2,1)S(1)} collective-permute-done((bf16[160,9,160]{2,0,1:T(8,128)(2,1)S(1)}, bf16[160,9,160]{2,0,1:T(8,128)(2,1)S(1)}, u32[]{:S(2)}, u32[]{:S(2)}) %collective-permute-start) | collective-permute-done | bytes 460832 | tf_op jit(solution)/shard_map/ppermute | solution.py:38
  275.8 13.9 %collective-permute-done.1 = bf16[160,9,160]{2,0,1:T(8,128)(2,1)S(1)} collective-permute-done((bf16[160,9,160]{2,0,1:T(8,128)(2,1)S(1)}, bf16[160,9,160]{2,0,1:T(8,128)(2,1)S(1)}, u32[]{:S(2)}, u32[]{:S(2)}) %collective-permute-start.1) | collective-permute-done | bytes 460832 | tf_op jit(solution)/shard_map/ppermute | solution.py:38
  289.7 2.2 collective-permute-done.2
  292.0 2.2 pad_maximum_fusion
  294.1 2.4 gather_fusion
  296.6 6.2 %copy.34 = bf16[4,160,9,160]{1,0,3,2:T(4,128)(2,1)S(1)} copy(bf16[4,160,9,160]{3,1,2,0:T(8,128)(2,1)} %gather_fusion) | data formatting | bytes 3686400 | tf_op jit(solution)/shard_map/jit(_take)/gather | solution.py:45
  302.8 3.0 reshape.482
  305.7 11.5 %convolution_bitcast_fusion = f32[32,9,160,8,8]{2,4,3,0,1:T(8,128)S(1)} fusion(bf16[32,160,64]{1,2,0:T(8,128)(2,1)} %collective-permute-done.11, bf16[32,160,64]{1,2,0:T(8,128)(2,1)} %collective-permute-done.10, bf16[32,160,64]{1,2,0:T(8,128)(2,1)} %collective-permute-done.9, bf16[32,160,64]{1,2,0:T(8,128)(2,1)} %multiply_convert_fusion.1, ...), kind=kOutput, calls=%fused_computation.23 | convolution fusion | flops 3785359360 | bytes 16261120 | tf_op jit(solution)/shard_map/scq,cte->steq/dot_general | solution.py:60
  317.2 2.4 fusion.74
  322.2 4.3 all-to-all-start.2
  326.5 3.5 gather_fusion.4
  330.1 1.8 broadcast_select_fusion
  331.9 9.1 %all-to-all-done.2 = bf16[32,160,64]{1,2,0:T(8,128)(2,1)} async-done(((bf16[32,160,64]{1,2,0:T(8,128)(2,1)}), bf16[32,160,64]{1,2,0:T(8,128)(2,1)}, u32[]{:S(2)}, u32[]{:S(2)}) %all-to-all-start.2) | async-done | bytes 655392 | tf_op jit(solution)/shard_map/all_to_all | solution.py:176
  341.0 3.7 all-to-all-start.1
  344.7 2.0 collective-permute-start.16
  346.8 1.9 collective-permute-start.17
  348.8 2.7 collective-permute-start.13
  352.6 1.6 collective-permute-start.14
  354.3 9.2 %collective-permute-done.16 = bf16[160,640]{1,0:T(8,128)(2,1)S(1)} collective-permute-done((bf16[160,640]{1,0:T(8,128)(2,1)S(1)}, bf16[160,640]{1,0:T(8,128)(2,1)S(1)}, u32[]{:S(2)}, u32[]{:S(2)}) %collective-permute-start.16) | collective-permute-done | bytes 204832 | tf_op jit(solution)/shard_map/ppermute | solution.py:38
  363.4 11.0 %collective-permute-done.17 = bf16[160,640]{1,0:T(8,128)(2,1)S(1)} collective-permute-done((bf16[160,640]{1,0:T(8,128)(2,1)S(1)}, bf16[160,640]{1,0:T(8,128)(2,1)S(1)}, u32[]{:S(2)}, u32[]{:S(2)}) %collective-permute-start.17) | collective-permute-done | bytes 204832 | tf_op jit(solution)/shard_map/ppermute | solution.py:38
  378.0 2.8 collective-permute-done.13
  380.8 2.5 collective-permute-done.14
  383.3 2.2 pad_maximum_fusion.4
  385.5 1.8 gather_fusion.2
  387.4 3.1 fusion.50
  390.5 2.3 copy.41
  394.7 2.1 fusion.80
  396.8 1.9 fusion.79
  398.7 11.1 %convolution_convert_fusion = bf16[8,10,64,64]{3,2,1,0:T(8,128)(2,1)S(1)} fusion(bf16[8,10,64,128]{3,2,1,0:T(8,128)(2,1)} %bitcast.149, f32[8,10,64]{2,1,0:T(8,128)S(1)} %fusion.79, f32[8,10,64,128]{3,2,1,0:T(8,128)} %fusion.80, pred[8,128]{1,0:T(8,128)(4,1)S(1)} %iota_compare_fusion.4), kind=kOutput, calls=%fused_computation.87 | convolution fusion | flops 87495808 | bytes 4609024 | tf_op jit(solution)/shard_map/shqk,shdk->shdq/dot_general | solution.py:199
  411.9 17.5 %all_to_all.43 = bf16[4,8,160,64]{2,3,1,0:T(8,128)(2,1)S(1)} all-to-all(bf16[4,8,160,64]{2,3,1,0:T(8,128)(2,1)S(1)} %pad_maximum_fusion.2), channel_id=1, replica_groups=mesh['groups'=2,'dp'=4,'mp'=4] {'mp'}, dimensions={0} | all-to-all | bytes 1310720 | tf_op jit(solution)/shard_map/all_to_all | solution.py:207
  (140 shorter events, 26.3 us)
Async XLA Ops:
  0.0 2.3 copy-start
  11.3 5.5 %copy-start.4 = (bf16[32,160,64]{1,2,0:T(8,128)(2,1)S(1)}, bf16[32,160,64]{1,2,0:T(8,128)(2,1)}, u32[]{:S(2)}) copy-start(bf16[32,160,64]{1,2,0:T(8,128)(2,1)} %param.10) | copy-start | bytes 1966084
  11.3 310.9 %all-to-all-start = ((bf16[4,16,320,128]{3,2,1,0:T(8,128)(2,1)}), bf16[4,16,320,128]{3,2,1,0:T(8,128)(2,1)}, u32[]{:S(2)}, u32[]{:S(2)}) async-start(bf16[4,16,320,128]{3,2,1,0:T(8,128)(2,1)} %select_select_fusion), calls=%async_computation | async-start | bytes 10485760 | tf_op jit(solution)/shard_map/all_to_all | solution.py:117
  17.3 4.3 copy-start.7
  17.3 8.7 %copy-start.18 = (bf16[32,2,160]{2,1,0:T(2,128)(2,1)S(1)}, bf16[32,2,160]{2,1,0:T(2,128)(2,1)}, u32[]{:S(2)}) copy-start(bf16[32,2,160]{2,1,0:T(2,128)(2,1)} %param.11) | copy-start | bytes 61444
  19.9 25.0 %collective-permute-start.7 = (bf16[32,160,64]{1,2,0:T(8,128)(2,1)}, bf16[32,160,64]{1,2,0:T(8,128)(2,1)}, u32[]{:S(2)}, u32[]{:S(2)}) collective-permute-start(bf16[32,160,64]{1,2,0:T(8,128)(2,1)} %fusion.36), channel_id=1, source_target_pairs={{0,2},{1,3},{2,0},{3,1},{4,6},{5,7},{6,4},{7,5},{8,10},{9,11},{10,... | collective-permute-start | bytes 1966088 | tf_op jit(solution)/shard_map/ppermute | solution.py:29
  21.5 156.3 %collective-permute-start.3 = (bf16[160,9,160]{2,0,1:T(8,128)(2,1)S(1)}, bf16[160,9,160]{2,0,1:T(8,128)(2,1)S(1)}, u32[]{:S(2)}, u32[]{:S(2)}) collective-permute-start(bf16[160,9,160]{2,0,1:T(8,128)(2,1)S(1)} %copy-done.7), channel_id=1, source_target_pairs={{0,4},{4,8},{8,12},{12,0},{1,5},{5,9},{9,13},{13,1},{2,6},{6,10},{... | collective-permute-start | bytes 1382408 | tf_op jit(solution)/shard_map/ppermute | solution.py:38
  23.0 169.5 %collective-permute-start.4 = (bf16[160,9,160]{2,0,1:T(8,128)(2,1)S(1)}, bf16[160,9,160]{2,0,1:T(8,128)(2,1)S(1)}, u32[]{:S(2)}, u32[]{:S(2)}) collective-permute-start(bf16[160,9,160]{2,0,1:T(8,128)(2,1)S(1)} %copy-done.7), channel_id=1, source_target_pairs={{0,8},{4,12},{8,0},{12,4},{1,9},{5,13},{9,1},{13,5},{2,10},{6,14},... | collective-permute-start | bytes 1382408 | tf_op jit(solution)/shard_map/ppermute | solution.py:38
  23.9 170.6 %collective-permute-start.5 = (bf16[160,9,160]{2,0,1:T(8,128)(2,1)S(1)}, bf16[160,9,160]{2,0,1:T(8,128)(2,1)S(1)}, u32[]{:S(2)}, u32[]{:S(2)}) collective-permute-start(bf16[160,9,160]{2,0,1:T(8,128)(2,1)S(1)} %copy-done.7), channel_id=1, source_target_pairs={{0,12},{4,0},{8,4},{12,8},{1,13},{5,1},{9,5},{13,9},{2,14},{6,2},{... | collective-permute-start | bytes 1382408 | tf_op jit(solution)/shard_map/ppermute | solution.py:38
  25.9 183.3 %collective-permute-start.6 = (bf16[32,160,64]{1,2,0:T(8,128)(2,1)}, bf16[32,160,64]{1,2,0:T(8,128)(2,1)}, u32[]{:S(2)}, u32[]{:S(2)}) collective-permute-start(bf16[32,160,64]{1,2,0:T(8,128)(2,1)} %fusion.36), channel_id=1, source_target_pairs={{0,1},{1,0},{2,3},{3,2},{4,5},{5,4},{6,7},{7,6},{8,9},{9,8},{10,11... | collective-permute-start | bytes 1966088 | tf_op jit(solution)/shard_map/ppermute | solution.py:30
  44.9 164.3 %collective-permute-start.8 = (bf16[32,160,64]{1,2,0:T(8,128)(2,1)}, bf16[32,160,64]{1,2,0:T(8,128)(2,1)}, u32[]{:S(2)}, u32[]{:S(2)}) collective-permute-start(bf16[32,160,64]{1,2,0:T(8,128)(2,1)} %collective-permute-done.7), channel_id=1, source_target_pairs={{0,1},{1,0},{2,3},{3,2},{4,5},{5,4},{6,7},{7,6},{8,9},{9,8},{10,11... | collective-permute-start | bytes 1966088 | tf_op jit(solution)/shard_map/ppermute | solution.py:31
  177.8 16.7 %copy-start.11 = (bf16[160,9,160]{2,0,1:T(8,128)(2,1)}, bf16[160,9,160]{2,0,1:T(8,128)(2,1)S(1)}, u32[]{:S(2)}) copy-start(bf16[160,9,160]{2,0,1:T(8,128)(2,1)S(1)} %collective-permute-done.3) | copy-start | bytes 1382404
  192.5 2.1 copy-start.12
  194.5 0.9 copy-start.13
  223.7 3.7 copy-start.8
  223.7 7.4 %copy-start.19 = (s32[128]{0:T(128)S(1)}, s32[128]{0:T(128)}, u32[]{:S(2)}) copy-start(s32[128]{0:T(128)} %param.18) | copy-start | bytes 1540
  223.7 26.9 %copy-start.20 = (s32[128]{0:T(128)S(1)}, s32[128]{0:T(128)}, u32[]{:S(2)}) copy-start(s32[128]{0:T(128)} %param.17) | copy-start | bytes 1540
  225.9 24.5 %collective-permute-start.10 = (bf16[32,160,64]{1,2,0:T(8,128)(2,1)}, bf16[32,160,64]{1,2,0:T(8,128)(2,1)}, u32[]{:S(2)}, u32[]{:S(2)}) collective-permute-start(bf16[32,160,64]{1,2,0:T(8,128)(2,1)} %multiply_convert_fusion.1), channel_id=1, source_target_pairs={{0,2},{1,3},{2,0},{3,1},{4,6},{5,7},{6,4},{7,5},{8,10},{9,11},{10,... | collective-permute-start | bytes 1966088 | tf_op jit(solution)/shard_map/ppermute | solution.py:29
  227.4 48.4 %collective-permute-start = (bf16[160,9,160]{2,0,1:T(8,128)(2,1)S(1)}, bf16[160,9,160]{2,0,1:T(8,128)(2,1)S(1)}, u32[]{:S(2)}, u32[]{:S(2)}) collective-permute-start(bf16[160,9,160]{2,0,1:T(8,128)(2,1)S(1)} %copy-done.8), channel_id=1, source_target_pairs={{0,4},{4,8},{8,12},{12,0},{1,5},{5,9},{9,13},{13,1},{2,6},{6,10},{... | collective-permute-start | bytes 1382408 | tf_op jit(solution)/shard_map/ppermute | solution.py:38
  227.4 62.3 %collective-permute-start.1 = (bf16[160,9,160]{2,0,1:T(8,128)(2,1)S(1)}, bf16[160,9,160]{2,0,1:T(8,128)(2,1)S(1)}, u32[]{:S(2)}, u32[]{:S(2)}) collective-permute-start(bf16[160,9,160]{2,0,1:T(8,128)(2,1)S(1)} %copy-done.8), channel_id=1, source_target_pairs={{0,8},{4,12},{8,0},{12,4},{1,9},{5,13},{9,1},{13,5},{2,10},{6,14},... | collective-permute-start | bytes 1382408 | tf_op jit(solution)/shard_map/ppermute | solution.py:38
  229.1 62.9 %collective-permute-start.2 = (bf16[160,9,160]{2,0,1:T(8,128)(2,1)S(1)}, bf16[160,9,160]{2,0,1:T(8,128)(2,1)}, u32[]{:S(2)}, u32[]{:S(2)}) collective-permute-start(bf16[160,9,160]{2,0,1:T(8,128)(2,1)S(1)} %copy-done.8), channel_id=1, source_target_pairs={{0,12},{4,0},{8,4},{12,8},{1,13},{5,1},{9,5},{13,9},{2,14},{6,2},{... | collective-permute-start | bytes 1382408 | tf_op jit(solution)/shard_map/ppermute | solution.py:38
  231.4 74.4 %collective-permute-start.9 = (bf16[32,160,64]{1,2,0:T(8,128)(2,1)}, bf16[32,160,64]{1,2,0:T(8,128)(2,1)}, u32[]{:S(2)}, u32[]{:S(2)}) collective-permute-start(bf16[32,160,64]{1,2,0:T(8,128)(2,1)} %multiply_convert_fusion.1), channel_id=1, source_target_pairs={{0,1},{1,0},{2,3},{3,2},{4,5},{5,4},{6,7},{7,6},{8,9},{9,8},{10,11... | collective-permute-start | bytes 1966088 | tf_op jit(solution)/shard_map/ppermute | solution.py:30
  250.4 55.4 %collective-permute-start.11 = (bf16[32,160,64]{1,2,0:T(8,128)(2,1)}, bf16[32,160,64]{1,2,0:T(8,128)(2,1)}, u32[]{:S(2)}, u32[]{:S(2)}) collective-permute-start(bf16[32,160,64]{1,2,0:T(8,128)(2,1)} %collective-permute-done.10), channel_id=1, source_target_pairs={{0,1},{1,0},{2,3},{3,2},{4,5},{5,4},{6,7},{7,6},{8,9},{9,8},{10,11... | collective-permute-start | bytes 1966088 | tf_op jit(solution)/shard_map/ppermute | solution.py:31
  275.8 16.2 %copy-start.9 = (bf16[160,9,160]{2,0,1:T(8,128)(2,1)}, bf16[160,9,160]{2,0,1:T(8,128)(2,1)S(1)}, u32[]{:S(2)}) copy-start(bf16[160,9,160]{2,0,1:T(8,128)(2,1)S(1)} %collective-permute-done) | copy-start | bytes 1382404
  289.7 2.2 copy-start.10
  305.7 11.5 %copy-start.5 = (bf16[32,160,64]{1,2,0:T(8,128)(2,1)S(1)}, bf16[32,160,64]{1,2,0:T(8,128)(2,1)}, u32[]{:S(2)}) copy-start(bf16[32,160,64]{1,2,0:T(8,128)(2,1)} %param.10) | copy-start | bytes 1966084
  319.7 2.6 copy-start.2
  322.2 18.8 %all-to-all-start.2 = ((bf16[32,160,64]{1,2,0:T(8,128)(2,1)}), bf16[32,160,64]{1,2,0:T(8,128)(2,1)}, u32[]{:S(2)}, u32[]{:S(2)}) async-start(bf16[32,160,64]{1,2,0:T(8,128)(2,1)} %multiply_convert_fusion), calls=%async_computation.2 | async-start | bytes 2097152 | tf_op jit(solution)/shard_map/all_to_all | solution.py:176
  331.9 12.8 %copy-start.14 = (bf16[160,640]{1,0:T(8,128)(2,1)S(1)}, bf16[160,640]{1,0:T(8,128)(2,1)}, u32[]{:S(2)}) copy-start(bf16[160,640]{1,0:T(8,128)(2,1)} %param.15) | copy-start | bytes 614404
  331.9 19.7 %copy-start.21 = (s32[168]{0:T(256)S(1)}, s32[168]{0:T(256)}, u32[]{:S(2)}) copy-start(s32[168]{0:T(256)} %param.19) | copy-start | bytes 2020
  341.0 51.8 %all-to-all-start.1 = ((bf16[32,320,128]{2,1,0:T(8,128)(2,1)}), bf16[32,320,128]{2,1,0:T(8,128)(2,1)S(1)}, u32[]{:S(2)}, u32[]{:S(2)}) async-start(bf16[32,320,128]{2,1,0:T(8,128)(2,1)} %broadcast_select_fusion), calls=%async_computation.1 | async-start | bytes 5242880 | tf_op jit(solution)/shard_map/all_to_all | solution.py:177
  344.7 7.9 %collective-permute-start.15 = (bf16[160,640]{1,0:T(8,128)(2,1)S(1)}, bf16[160,640]{1,0:T(8,128)(2,1)S(1)}, u32[]{:S(2)}, u32[]{:S(2)}) collective-permute-start(bf16[160,640]{1,0:T(8,128)(2,1)S(1)} %copy-done.14), channel_id=1, source_target_pairs={{0,4},{4,8},{8,12},{12,0},{1,5},{5,9},{9,13},{13,1},{2,6},{6,10},{... | collective-permute-start | bytes 614408 | tf_op jit(solution)/shard_map/ppermute | solution.py:38
  344.7 18.7 %collective-permute-start.16 = (bf16[160,640]{1,0:T(8,128)(2,1)S(1)}, bf16[160,640]{1,0:T(8,128)(2,1)S(1)}, u32[]{:S(2)}, u32[]{:S(2)}) collective-permute-start(bf16[160,640]{1,0:T(8,128)(2,1)S(1)} %copy-done.14), channel_id=1, source_target_pairs={{0,8},{4,12},{8,0},{12,4},{1,9},{5,13},{9,1},{13,5},{2,10},{6,14},... | collective-permute-start | bytes 614408 | tf_op jit(solution)/shard_map/ppermute | solution.py:38
  346.8 27.7 %collective-permute-start.17 = (bf16[160,640]{1,0:T(8,128)(2,1)S(1)}, bf16[160,640]{1,0:T(8,128)(2,1)S(1)}, u32[]{:S(2)}, u32[]{:S(2)}) collective-permute-start(bf16[160,640]{1,0:T(8,128)(2,1)S(1)} %copy-done.14), channel_id=1, source_target_pairs={{0,12},{4,0},{8,4},{12,8},{1,13},{5,1},{9,5},{13,9},{2,14},{6,2},{... | collective-permute-start | bytes 614408 | tf_op jit(solution)/shard_map/ppermute | solution.py:38
  348.7 29.3 %collective-permute-start.12 = (bf16[160,640]{1,0:T(8,128)(2,1)}, bf16[160,640]{1,0:T(8,128)(2,1)}, u32[]{:S(2)}, u32[]{:S(2)}) collective-permute-start(bf16[160,640]{1,0:T(8,128)(2,1)} %param.16), channel_id=1, source_target_pairs={{0,4},{4,8},{8,12},{12,0},{1,5},{5,9},{9,13},{13,1},{2,6},{6,10},{... | collective-permute-start | bytes 614408 | tf_op jit(solution)/shard_map/ppermute | solution.py:38
  348.8 32.0 %collective-permute-start.13 = (bf16[160,640]{1,0:T(8,128)(2,1)}, bf16[160,640]{1,0:T(8,128)(2,1)}, u32[]{:S(2)}, u32[]{:S(2)}) collective-permute-start(bf16[160,640]{1,0:T(8,128)(2,1)} %param.16), channel_id=1, source_target_pairs={{0,8},{4,12},{8,0},{12,4},{1,9},{5,13},{9,1},{13,5},{2,10},{6,14},... | collective-permute-start | bytes 614408 | tf_op jit(solution)/shard_map/ppermute | solution.py:38
  352.6 21.9 %copy-start.15 = (bf16[160,640]{1,0:T(8,128)(2,1)}, bf16[160,640]{1,0:T(8,128)(2,1)S(1)}, u32[]{:S(2)}) copy-start(bf16[160,640]{1,0:T(8,128)(2,1)S(1)} %collective-permute-done.15) | copy-start | bytes 614404
  352.6 30.7 %collective-permute-start.14 = (bf16[160,640]{1,0:T(8,128)(2,1)}, bf16[160,640]{1,0:T(8,128)(2,1)}, u32[]{:S(2)}, u32[]{:S(2)}) collective-permute-start(bf16[160,640]{1,0:T(8,128)(2,1)} %param.16), channel_id=1, source_target_pairs={{0,12},{4,0},{8,4},{12,8},{1,13},{5,1},{9,5},{13,9},{2,14},{6,2},{... | collective-permute-start | bytes 614408 | tf_op jit(solution)/shard_map/ppermute | solution.py:38
  363.4 11.1 %copy-start.16 = (bf16[160,640]{1,0:T(8,128)(2,1)}, bf16[160,640]{1,0:T(8,128)(2,1)S(1)}, u32[]{:S(2)}) copy-start(bf16[160,640]{1,0:T(8,128)(2,1)S(1)} %collective-permute-done.16) | copy-start | bytes 614404
  374.5 0.7 copy-start.17
  393.0 1.7 copy-start.6
  411.7 17.7 %copy-start.3 = (f32[32,160,64]{1,2,0:T(8,128)S(1)}, f32[32,160,64]{1,2,0:T(8,128)}, u32[]{:S(2)}) copy-start(f32[32,160,64]{1,2,0:T(8,128)} %copy-done.2) | copy-start | bytes 3932164
  411.9 18.9 %copy-start.1 = (bf16[42,320,128]{2,1,0:T(8,128)(2,1)S(1)}, bf16[42,320,128]{2,1,0:T(8,128)(2,1)}, u32[]{:S(2)}) copy-start(bf16[42,320,128]{2,1,0:T(8,128)(2,1)} %param.14) | copy-start | bytes 10321924
